TPU v7x, 512 devices: a whole 4x4x16 slice. The times are simulated.
512 devices in a mesh: dp: 32 (over x, y, core), expert: 16 (over z).
Axes of the slice: x: 4, y: 4, z: 16, core: 2. Of those that a mesh axis runs over, the one named last changes fastest.
Arguments:
- out_grad: bfloat16 [65536, 2048], P(('dp', 'expert')), may hold values from -6 to 6
- expert_ids: int32 [65536, 4], P(('dp', 'expert')), may hold values from 0 to 15, all different within a row; in each aligned block of 128 rows (0 to 127, 128 to 255, ...) at most 64 rows name the same one
- route_weights: bfloat16 [65536, 4], P(('dp', 'expert')), may hold values from 0.049804688 to 1
- pre_activations: bfloat16 [65536, 4, 1536], P(('dp', 'expert')), may hold values from -6 to 6
- down_weight: bfloat16 [16, 768, 2048], P('expert', 'dp'), may hold values from -0.21875 to 0.21875
Outputs:
- pre_grad: bfloat16 [65536, 4, 1536], P(('dp', 'expert'))
- weight_grad: bfloat16 [65536, 4], P(('dp', 'expert'))
- down_grad: bfloat16 [16, 768, 2048], P('expert', 'dp')
Inputs may be any that keep to these rules, and one draw needn't show every extreme that they name: `expert_ids`: among the 128 rows of one device, each expert is named by at most 64 rows, a bound that some block reaches; the numbers in a row are distinct.
All inputs are finite; a program needn't handle non-finite values.
Results may differ from a plain program's by a relative error of at most 0.015.
Values may be sent and summed in bfloat16 or wider, within the bound.
No kernel may reach another device: no remote copies, remote signals or barrier semaphores. Data moves between devices by JAX's collectives and lax.ppermute only.
A program may use at most 64 MiB of HBM per device.

v0:
```python
import jax
import jax.numpy as jnp
from jax import lax
from jax.sharding import PartitionSpec as P

F32 = jnp.float32
BF16 = jnp.bfloat16


def body(out_grad, expert_ids, route_weights, pre_activations, down_weight):
    tok, width = out_grad.shape
    top = expert_ids.shape[1]
    units = pre_activations.shape[2] // 2
    ndp = lax.axis_size("dp")
    rows = down_weight.shape[1]
    n_all = ndp * tok
    nex = lax.axis_size("expert")
    w_all = lax.all_to_all(
        jnp.broadcast_to(down_weight, (nex,) + down_weight.shape[1:]), "expert", 0, 0, tiled=True
    )
    experts = w_all.shape[0]
    wcat = w_all.reshape(experts * rows, width)
    og_all = lax.all_gather(out_grad, "dp", axis=0, tiled=True)
    gate = pre_activations[..., :units].astype(F32)
    up = pre_activations[..., units:].astype(F32)
    sig = jax.nn.sigmoid(gate)
    hidden = (gate * sig * up).astype(BF16)
    send_h = hidden.reshape(tok, top, ndp, rows).transpose(2, 1, 3, 0)
    meta = jnp.stack([expert_ids.T.astype(BF16), route_weights.T], axis=1)
    send_h = jnp.concatenate([send_h, jnp.broadcast_to(meta[None], (ndp, top, 2, tok))], axis=2)
    got_h = lax.all_to_all(send_h, "dp", 0, 0, tiled=True)
    got_h = got_h.transpose(1, 2, 0, 3).reshape(top, rows + 2, n_all)
    hid_t = got_h[:, :rows].astype(F32)
    ids_t = got_h[:, rows].astype(F32)
    rw_t = got_h[:, rows + 1].astype(F32)
    eidx = jnp.arange(experts, dtype=F32)[:, None, None]
    hp = jnp.zeros((experts, rows, n_all), F32)
    for k in range(top):
        hp = hp + jnp.where(
            ids_t[k][None, None, :] == eidx, (rw_t[k][None, :] * hid_t[k])[None], 0.0
        )
    hp = hp.reshape(experts * rows, n_all).astype(BF16)
    part = lax.dot_general(hp, og_all, (((1,), (0,)), ((), ())), preferred_element_type=F32)
    part = (part / ndp).reshape(experts, rows, width).astype(BF16)
    down_grad = lax.psum_scatter(part, "expert", scatter_dimension=0, tiled=True)
    _, wcat = lax.optimization_barrier((part, wcat))
    r_t = lax.dot_general(wcat, og_all, (((1,), (1,)), ((), ())), preferred_element_type=F32)
    r_t = r_t.reshape(experts, rows, n_all)
    hg_t = jnp.stack(
        [jnp.sum(jnp.where(ids_t[k][None, None, :] == eidx, r_t, 0.0), axis=0) for k in range(top)]
    ).astype(BF16)
    send_g = hg_t.reshape(top, rows, ndp, tok).transpose(2, 0, 1, 3)
    got_g = lax.all_to_all(send_g, "dp", 0, 0, tiled=True)
    hidden_grad = got_g.transpose(3, 1, 0, 2).reshape(tok, top, units)
    hg32 = hidden_grad.astype(F32)
    weight_grad = jnp.sum(hg32 * hidden.astype(F32), axis=-1).astype(BF16)
    cot = route_weights.astype(F32)[..., None] * hg32
    gate_grad = cot * up * sig * (1.0 + gate * (1.0 - sig))
    up_grad = cot * gate * sig
    pre_grad = jnp.concatenate([gate_grad, up_grad], axis=-1).astype(BF16)
    return (pre_grad, weight_grad, down_grad)


def solution(mesh):
    return jax.shard_map(
        body,
        mesh=mesh,
        in_specs=(
            P(("dp", "expert"), None),
            P(("dp", "expert"), None),
            P(("dp", "expert"), None),
            P(("dp", "expert"), None, None),
            P("expert", "dp", None),
        ),
        out_specs=(
            P(("dp", "expert"), None, None),
            P(("dp", "expert"), None),
            P("expert", "dp", None),
        ),
        check_vma=False,
    )
```

profile of v0, /device:TPU:2, one launch (start us, length us, event | category | flops | bytes accessed | tf_op | source)
XLA Modules:
  0.0 194.8 jit_solution(4540025526134113326)
XLA Ops:
  7.2 0.7 all-gather.2.cloned.1.call-update
  7.9 1.9 fusion.11
  9.8 0.7 copy.28
  10.5 0.7 copy.29
  11.2 0.5 fusion
  11.8 0.1 pad_maximum_fusion.1
  11.9 0.7 copy.19
  12.6 21.3 %all_to_all.15 = bf16[32,4,26,128]{3,1,2,0:T(4,128)(2,1)S(1)} all-to-all(bf16[32,4,26,128]{3,1,2,0:T(4,128)(2,1)S(1)} %copy.19), channel_id=1, replica_groups=mesh['dp'=32,'expert'=16] {'dp'}, dimensions={0} | all-to-all | bytes 1703936 | tf_op jit(solution)/shard_map/all_to_all | solution.py:31
  33.9 1.3 broadcast_in_dim.115
  35.3 14.0 %all-to-all-start.1 = ((bf16[16,24,2048]{2,1,0:T(8,128)(2,1)}), bf16[16,24,2048]{2,1,0:T(8,128)(2,1)}, u32[]{:S(2)}, u32[]{:S(2)}) async-start(bf16[16,24,2048]{2,1,0:T(8,128)(2,1)} %broadcast_in_dim.115), calls=%async_computation.1 | async-start | bytes 3145728 | tf_op jit(solution)/shard_map/all_to_all | solution.py:18
  49.3 0.4 copy_bitcast_fusion
  49.8 0.1 fusion.12
  49.9 0.2 slice_convert_fusion
  50.1 1.8 slice_multiply_fusion.3
  51.9 0.2 copy.43
  52.2 0.2 copy.44
  52.4 0.2 copy.45
  52.6 0.2 copy.46
  53.0 4.3 %add_convert_fusion = bf16[16,24,4096]{2,1,0:T(8,128)(2,1)} fusion(f32[24,4096]{1,0:T(8,128)S(1)} %bitcast.82, f32[24,4096]{1,0:T(8,128)S(1)} %bitcast.83, f32[24,4096]{1,0:T(8,128)S(1)} %bitcast.84, f32[24,4096]{1,0:T(8,128)S(1)} %bitcast.85, pred[16,4096]{1,0:T(8,128)(4,1)S(1)} %iota_compare_fusion, pred[16,4096]{1,0:T(8,128)(4,1)S(1)} %iota_compare_fusion.1, ...), kind=kLoop, calls=%fused_computation.4 | loop fusion | flops 12582912 | bytes 4980736 | tf_op jit(solution)/shard_map/convert.12
  57.3 46.1 %all-gather.2.cloned.1.call-done = bf16[4096,2048]{1,0:T(8,128)(2,1)} async-done(((bf16[128,2048]{1,0:T(8,128)(2,1)}), bf16[4096,2048]{1,0:T(8,128)(2,1)}) %all-gather.2.cloned.1.call-update) | async-done | bytes 16777232 | tf_op jit(solution)/shard_map/all_gather | solution.py:23
  103.4 12.0 %multiply_convert_fusion = bf16[384,2048]{1,0:T(8,128)(2,1)} fusion(bf16[384,4096]{1,0:T(8,128)(2,1)} %bitcast.80, bf16[4096,2048]{1,0:T(8,128)(2,1)} %all-gather.2.cloned.1.call-done), kind=kOutput, calls=%fused_computation.5 | convolution fusion | flops 6444023808 | bytes 21495808 | tf_op jit(solution)/shard_map/dot_general | solution.py:43
  115.5 5.9 %all-to-all-done.1 = bf16[16,24,2048]{2,1,0:T(8,128)(2,1)} async-done(((bf16[16,24,2048]{2,1,0:T(8,128)(2,1)}), bf16[16,24,2048]{2,1,0:T(8,128)(2,1)}, u32[]{:S(2)}, u32[]{:S(2)}) %all-to-all-start.1) | async-done | bytes 1572896 | tf_op jit(solution)/shard_map/all_to_all | solution.py:18
  121.4 10.7 %fusion.14 = f32[384,4096]{1,0:T(8,128)S(1)} fusion(bf16[384,2048]{1,0:T(8,128)(2,1)} %bitcast.18, bf16[4096,2048]{1,0:T(8,128)(2,1)} %all-gather.2.cloned.1.call-done), kind=kOutput, calls=%fused_computation.53 | convolution fusion | flops 6442450944 | bytes 24641536 | tf_op jit(solution)/shard_map/dot_general | solution.py:47
  132.1 3.4 %select_reduce_fusion.3 = (bf16[24,4096]{1,0:T(8,128)(2,1)S(1)}, bf16[24,4096]{1,0:T(8,128)(2,1)S(1)}, bf16[24,4096]{1,0:T(8,128)(2,1)S(1)}, bf16[24,4096]{1,0:T(8,128)(2,1)S(1)}) fusion(f32[16,24,4096]{2,1,0:T(8,128)S(1)} %bitcast.79, pred[16,4096]{1,0:T(8,128)(4,1)S(1)} %iota_compare_fusion.3, pred[16,4096]{1,0:T(8,128)(4,1)S(1)} %iota_compare_fusion, ...), kind=kLoop, calls=%fused_computation.3 | loop fusion | flops 12189696 | bytes 7340032 | tf_op jit(solution)/shard_map/reduce_sum | solution.py:50
  135.6 0.1 maximum_bitcast_fusion
  135.8 1.2 copy.21
  136.9 8.1 %all-to-all-start.2 = ((bf16[32,4,24,128]{3,2,1,0:T(8,128)(2,1)}), bf16[32,4,24,128]{3,2,1,0:T(8,128)(2,1)S(1)}, u32[]{:S(2)}, u32[]{:S(2)}) async-start(bf16[32,4,24,128]{3,2,1,0:T(8,128)(2,1)} %copy.21), calls=%async_computation.2 | async-start | bytes 1572864 | tf_op jit(solution)/shard_map/all_to_all | solution.py:53
  145.0 12.0 %all-to-all-done.2 = bf16[32,4,24,128]{3,2,1,0:T(8,128)(2,1)S(1)} async-done(((bf16[32,4,24,128]{3,2,1,0:T(8,128)(2,1)}), bf16[32,4,24,128]{3,2,1,0:T(8,128)(2,1)S(1)}, u32[]{:S(2)}, u32[]{:S(2)}) %all-to-all-start.2) | async-done | bytes 786464 | tf_op jit(solution)/shard_map/all_to_all | solution.py:53
  157.1 1.6 fusion.3
  158.7 0.1 pad_maximum_fusion
  158.8 2.5 %copy.23 = bf16[128,4,1536]{2,1,0:T(4,128)(2,1)} copy(bf16[128,4,1536]{0,2,1:T(8,128)(2,1)S(1)} %pad_maximum_fusion) | data formatting | bytes 3145728
  161.3 26.6 %reduce-scatter.2.cloned.1.call-done = bf16[1,24,2048]{2,1,0:T(8,128)(2,1)} async-done(((bf16[16,24,2048]{2,1,0:T(8,128)(2,1)}), bf16[1,24,2048]{2,1,0:T(8,128)(2,1)}) %reduce-scatter.2.cloned.1.call-update) | async-done | bytes 98320 | tf_op jit(solution)/shard_map/reduce_scatter | solution.py:45
  (23 shorter events, 0.5 us)
Async XLA Ops:
  7.2 96.3 %all-gather.2.cloned.1.call-start = ((), (), s32[]{:S(2)}) async-start(), calls=%async_computation.4 | async-start | bytes 17301504 | tf_op jit(solution)/shard_map/all_gather | solution.py:23
  9.8 1.4 copy-start.2
  9.8 1.4 copy-start.1
  11.9 22.0 %copy-start = (bf16[1,24,2048]{2,1,0:T(8,128)(2,1)S(1)}, bf16[1,24,2048]{2,1,0:T(8,128)(2,1)}, u32[]{:S(2)}) copy-start(bf16[1,24,2048]{2,1,0:T(8,128)(2,1)} %param.9) | copy-start | bytes 294916
  35.3 86.2 %all-to-all-start.1 = ((bf16[16,24,2048]{2,1,0:T(8,128)(2,1)}), bf16[16,24,2048]{2,1,0:T(8,128)(2,1)}, u32[]{:S(2)}, u32[]{:S(2)}) async-start(bf16[16,24,2048]{2,1,0:T(8,128)(2,1)} %broadcast_in_dim.115), calls=%async_computation.1 | async-start | bytes 3145728 | tf_op jit(solution)/shard_map/all_to_all | solution.py:18
  49.3 138.6 %reduce-scatter.2.cloned.1.call-start = ((), (), s32[]{:S(2)}) async-start(), calls=%async_computation.5 | async-start | bytes 1671168 | tf_op jit(solution)/shard_map/reduce_scatter | solution.py:45
  136.9 20.1 %all-to-all-start.2 = ((bf16[32,4,24,128]{3,2,1,0:T(8,128)(2,1)}), bf16[32,4,24,128]{3,2,1,0:T(8,128)(2,1)S(1)}, u32[]{:S(2)}, u32[]{:S(2)}) async-start(bf16[32,4,24,128]{3,2,1,0:T(8,128)(2,1)} %copy.21), calls=%async_computation.2 | async-start | bytes 1572864 | tf_op jit(solution)/shard_map/all_to_all | solution.py:53
Sparse Core Ops, SparseCore 0:
  11.1 92.2 all-gather.1
  115.6 72.2 reduce-scatter.1
where the time goes:
time: 195 us
  waiting for transfers between devices  91.4 us (47%)
  matrix products  22.7 us (12%)
  starting transfers between devices  22.2 us (11%)
  blocking collectives  21.3 us (11%)
  between operations  14.3 us (7%)
  other arithmetic  12.3 us (6%)
  local copies, waits for them, and re-layouts  10.5 us (5%)
    all_gather x1, waiting for transfers between devices, body(): og_all = lax.all_gather(out_grad, 'dp', axis=0, tiled=True)  46.1 us
    reduce_scatter x1, waiting for transfers between devices, body(): lax.psum_scatter(part, 'expert', scatter_dimension=0, tiled=True)  26.6 us
    all_to_all x1, blocking collectives, body(): got_h = lax.all_to_all(send_h, 'dp', 0, 0, tiled=True)  21.3 us
    all_to_all x1, starting transfers between devices, body(): lax.all_to_all(jnp.broadcast_to(down_weight, (nex,) + down_weight.shape[1...  14 us
    all_to_all x1, waiting for transfers between devices, body(): got_g = lax.all_to_all(send_g, 'dp', 0, 0, tiled=True)  12 us
    dot_general x1, matrix products, body(): lax.dot_general(hp, og_all, (((1,), (0,)), ((), ())), preferred_element_t...  12 us
    dot_general x1, matrix products, body(): lax.dot_general(wcat, og_all, (((1,), (1,)), ((), ())), preferred_element...  10.7 us
    all_to_all x1, starting transfers between devices, body(): got_g = lax.all_to_all(send_g, 'dp', 0, 0, tiled=True)  8.07 us
  transfers between devices with their start and end apart: 4, of which 4 were waited for; matrix products, arithmetic and copies ran while one was open for 23% of the time, Pallas kernels for 0%

commit v1 on v0

--- a/solution.py
+++ b/solution.py
@@ -20,7 +20,9 @@
     )
     experts = w_all.shape[0]
     wcat = w_all.reshape(experts * rows, width)
-    og_all = lax.all_gather(out_grad, "dp", axis=0, tiled=True)
+    og_all = jnp.concatenate(
+        lax.all_to_all(jnp.stack([out_grad] * lax.axis_size("dp")), "dp", 0, 0), axis=0
+    )
     gate = pre_activations[..., :units].astype(F32)
     up = pre_activations[..., units:].astype(F32)
     sig = jax.nn.sigmoid(gate)

time: 195 us -> 456 us (2.34)
  the two profiles are of different devices: /device:TPU:2 before, /device:TPU:1 now
where the time goes in v1:
time: 456 us; the launch traced here: 455 us
  waiting for transfers between devices  289 us (63%)
  starting transfers between devices  74.5 us (16%)
  blocking collectives  24.5 us (5%)
  matrix products  24.4 us (5%)
  local copies, waits for them, and re-layouts  19 us (4%)
  between operations  14.4 us (3%)
  other arithmetic  9.08 us (2%)
    all_to_all x1, waiting for transfers between devices, body(): lax.all_to_all(jnp.stack([out_grad] * lax.axis_size('dp')), 'dp', 0, 0)  227 us
    all_to_all x1, starting transfers between devices, body(): got_g = lax.all_to_all(send_g, 'dp', 0, 0, tiled=True)  56 us
    all_to_all x1, waiting for transfers between devices, body(): lax.all_to_all(jnp.broadcast_to(down_weight, (nex,) + down_weight.shape[1...  47.8 us
    all_to_all x1, blocking collectives, body(): got_h = lax.all_to_all(send_h, 'dp', 0, 0, tiled=True)  24.5 us
    all_to_all x1, waiting for transfers between devices, body(): got_g = lax.all_to_all(send_g, 'dp', 0, 0, tiled=True)  14.2 us
    all_to_all x1, starting transfers between devices, body(): lax.all_to_all(jnp.broadcast_to(down_weight, (nex,) + down_weight.shape[1...  13.4 us
    dot_general x1, matrix products, body(): lax.dot_general(wcat, og_all, (((1,), (1,)), ((), ())), preferred_element...  12.7 us
    dot_general x1, matrix products, body(): lax.dot_general(hp, og_all, (((1,), (0,)), ((), ())), preferred_element_t...  11.6 us
  transfers between devices with their start and end apart: 4, of which 3 were waited for; matrix products, arithmetic and copies ran while one was open for 9% of the time, Pallas kernels for 0%

profile of v1, /device:TPU:1, one launch (start us, length us, event | category | flops | bytes accessed | tf_op | source)
XLA Modules:
  0.0 455.1 jit_solution(16671607058256804401)
XLA Ops:
  7.2 1.9 fusion.11
  9.1 0.7 copy.29
  9.8 0.7 copy.30
  10.5 0.5 fusion
  11.0 0.1 pad_maximum_fusion.1
  11.2 0.7 copy.20
  11.9 24.5 %all_to_all.20 = bf16[32,4,26,128]{3,1,2,0:T(4,128)(2,1)S(1)} all-to-all(bf16[32,4,26,128]{3,1,2,0:T(4,128)(2,1)S(1)} %copy.20), channel_id=1, replica_groups=mesh['dp'=32,'expert'=16] {'dp'}, dimensions={0} | all-to-all | bytes 1703936 | tf_op jit(solution)/shard_map/all_to_all | solution.py:33
  36.4 5.9 %stack.21 = bf16[32,128,2048]{2,1,0:T(8,128)(2,1)} broadcast(bf16[128,2048]{1,0:T(8,128)(2,1)S(1)} %copy-done), dimensions={1,2} | broadcast | bytes 17301504 | tf_op jit(solution)/shard_map/stack | solution.py:24
  42.3 5.0 %all-to-all-start.1 = ((bf16[32,128,2048]{2,1,0:T(8,128)(2,1)}), bf16[32,128,2048]{2,1,0:T(8,128)(2,1)}, u32[]{:S(2)}, u32[]{:S(2)}) async-start(bf16[32,128,2048]{2,1,0:T(8,128)(2,1)} %stack.21), calls=%async_computation.1 | async-start | bytes 33554432 | tf_op jit(solution)/shard_map/all_to_all | solution.py:24
  47.2 0.4 copy_bitcast_fusion
  47.7 0.7 fusion.12
  48.4 0.2 slice_convert_fusion
  48.6 2.6 slice_multiply_fusion.3
  51.1 227.3 %all-to-all-done.1 = bf16[32,128,2048]{2,1,0:T(8,128)(2,1)} async-done(((bf16[32,128,2048]{2,1,0:T(8,128)(2,1)}), bf16[32,128,2048]{2,1,0:T(8,128)(2,1)}, u32[]{:S(2)}, u32[]{:S(2)}) %all-to-all-start.1) | async-done | bytes 16777248 | tf_op jit(solution)/shard_map/all_to_all | solution.py:24
  278.4 2.2 broadcast_in_dim.115
  280.7 13.4 %all-to-all-start.2 = ((bf16[16,24,2048]{2,1,0:T(8,128)(2,1)}), bf16[16,24,2048]{2,1,0:T(8,128)(2,1)}, u32[]{:S(2)}, u32[]{:S(2)}) async-start(bf16[16,24,2048]{2,1,0:T(8,128)(2,1)} %broadcast_in_dim.115), calls=%async_computation.2 | async-start | bytes 3145728 | tf_op jit(solution)/shard_map/all_to_all | solution.py:18
  294.0 0.2 reduce-scatter.2.cloned.1.call-start
  294.3 0.8 iota_compare_fusion
  295.1 1.3 copy.44
  296.3 0.2 copy.45
  296.6 0.2 copy.46
  296.8 0.2 copy.47
  297.2 3.0 add_convert_fusion
  300.2 11.6 %multiply_convert_fusion = bf16[384,2048]{1,0:T(8,128)(2,1)} fusion(bf16[384,4096]{1,0:T(8,128)(2,1)S(1)} %bitcast.82, bf16[4096,2048]{1,0:T(8,128)(2,1)} %bitcast.16), kind=kOutput, calls=%fused_computation.5 | convolution fusion | flops 6444023808 | bytes 21495808 | tf_op jit(solution)/shard_map/dot_general | solution.py:45
  311.9 47.8 %all-to-all-done.2 = bf16[16,24,2048]{2,1,0:T(8,128)(2,1)} async-done(((bf16[16,24,2048]{2,1,0:T(8,128)(2,1)}), bf16[16,24,2048]{2,1,0:T(8,128)(2,1)}, u32[]{:S(2)}, u32[]{:S(2)}) %all-to-all-start.2) | async-done | bytes 1572896 | tf_op jit(solution)/shard_map/all_to_all | solution.py:18
  359.6 12.7 %select_reduce_fusion.3 = (bf16[24,4096]{1,0:T(8,128)(2,1)S(1)}, bf16[24,4096]{1,0:T(8,128)(2,1)S(1)}, bf16[24,4096]{1,0:T(8,128)(2,1)S(1)}, bf16[24,4096]{1,0:T(8,128)(2,1)S(1)}) fusion(pred[16,4096]{1,0:T(8,128)(4,1)S(1)} %iota_compare_fusion.3, pred[16,4096]{1,0:T(8,128)(4,1)S(1)} %copy-done.2, pred[16,4096]{1,0:T(8,128)(4,1)S(1)} %iota_compare_fusion.1, ...), kind=kOutput, calls=%fused_computation.3 | convolution fusion | flops 6454640640 | bytes 19398656 | tf_op jit(solution)/shard_map/dot_general | solution.py:49
  372.5 0.1 maximum_bitcast_fusion
  372.6 1.2 copy.22
  373.8 56.0 %all-to-all-start.3 = ((bf16[32,4,24,128]{3,2,1,0:T(8,128)(2,1)}), bf16[32,4,24,128]{3,2,1,0:T(8,128)(2,1)S(1)}, u32[]{:S(2)}, u32[]{:S(2)}) async-start(bf16[32,4,24,128]{3,2,1,0:T(8,128)(2,1)} %copy.22), calls=%async_computation.3 | async-start | bytes 1572864 | tf_op jit(solution)/shard_map/all_to_all | solution.py:55
  429.8 14.2 %all-to-all-done.3 = bf16[32,4,24,128]{3,2,1,0:T(8,128)(2,1)S(1)} async-done(((bf16[32,4,24,128]{3,2,1,0:T(8,128)(2,1)}), bf16[32,4,24,128]{3,2,1,0:T(8,128)(2,1)S(1)}, u32[]{:S(2)}, u32[]{:S(2)}) %all-to-all-start.3) | async-done | bytes 786464 | tf_op jit(solution)/shard_map/all_to_all | solution.py:55
  444.0 1.6 fusion.3
  445.8 2.5 copy.24
  (32 shorter events, 0.5 us)
Async XLA Ops:
  9.1 1.4 copy-start.7
  9.1 1.4 copy-start.5
  11.2 25.2 %copy-start = (bf16[128,2048]{1,0:T(8,128)(2,1)S(1)}, bf16[128,2048]{1,0:T(8,128)(2,1)}, u32[]{:S(2)}) copy-start(bf16[128,2048]{1,0:T(8,128)(2,1)} %param.5) | copy-start | bytes 1572868
  42.3 236.2 %all-to-all-start.1 = ((bf16[32,128,2048]{2,1,0:T(8,128)(2,1)}), bf16[32,128,2048]{2,1,0:T(8,128)(2,1)}, u32[]{:S(2)}, u32[]{:S(2)}) async-start(bf16[32,128,2048]{2,1,0:T(8,128)(2,1)} %stack.21), calls=%async_computation.1 | async-start | bytes 33554432 | tf_op jit(solution)/shard_map/all_to_all | solution.py:24
  280.7 79.0 %all-to-all-start.2 = ((bf16[16,24,2048]{2,1,0:T(8,128)(2,1)}), bf16[16,24,2048]{2,1,0:T(8,128)(2,1)}, u32[]{:S(2)}, u32[]{:S(2)}) async-start(bf16[16,24,2048]{2,1,0:T(8,128)(2,1)} %broadcast_in_dim.115), calls=%async_computation.2 | async-start | bytes 3145728 | tf_op jit(solution)/shard_map/all_to_all | solution.py:18
  294.0 154.2 %reduce-scatter.2.cloned.1.call-start = ((), (), s32[]{:S(2)}) async-start(), calls=%async_computation.5 | async-start | bytes 1671168 | tf_op jit(solution)/shard_map/reduce_scatter | solution.py:47
  295.0 2.2 copy-start.1
  295.0 2.0 copy-start.4
  295.0 2.1 copy-start.3
  311.8 47.8 %copy-start.2 = (pred[16,4096]{1,0:T(8,128)(4,1)S(1)}, pred[16,4096]{1,0:T(8,128)(4,1)}, u32[]{:S(2)}) copy-start(pred[16,4096]{1,0:T(8,128)(4,1)} %copy-done.1) | copy-start | bytes 196612
  372.6 57.2 %copy-start.6 = (bf16[128,4]{0,1:T(4,128)(2,1)S(1)}, bf16[128,4]{0,1:T(4,128)(2,1)}, u32[]{:S(2)}) copy-start(bf16[128,4]{0,1:T(4,128)(2,1)} %param.7) | copy-start | bytes 3076
  373.8 70.2 %all-to-all-start.3 = ((bf16[32,4,24,128]{3,2,1,0:T(8,128)(2,1)}), bf16[32,4,24,128]{3,2,1,0:T(8,128)(2,1)S(1)}, u32[]{:S(2)}, u32[]{:S(2)}) async-start(bf16[32,4,24,128]{3,2,1,0:T(8,128)(2,1)} %copy.22), calls=%async_computation.3 | async-start | bytes 1572864 | tf_op jit(solution)/shard_map/all_to_all | solution.py:55
Sparse Core Ops, SparseCore 0:
  312.0 99.7 reduce-scatter.1
